TPU v7x, 512 devices: a whole 4x4x16 slice. The times are simulated.
512 devices in a mesh: mpo: 8 (over y, core), sec: 64 (over x, z).
Axes of the slice: x: 4, y: 4, z: 16, core: 2. Of those that a mesh axis runs over, the one named last changes fastest.
Arguments:
- theta: bfloat16 [16, 1024, 1024], P(None, 'sec'), may hold values from -6 to 6
- env_left: bfloat16 [24, 16384, 1024], P('mpo', 'sec'), may hold values from -0.1875 to 0.1875
- env_right: bfloat16 [24, 16384, 1024], P('mpo', 'sec'), may hold values from -0.0390625 to 0.0390625
- mpo_core: float32 [24, 24], replicated, may hold values from -1.25 to 1.25
- sector_sizes: int32 [16], replicated, may hold values from 1 to 1024, 12288 in all
Outputs:
- applied: bfloat16 [1024, 16384], P('mpo', 'sec')
Inputs may be any that keep to these rules, and one draw needn't show every extreme that they name: `sector_sizes`: one sector has exactly 1024 states in use; the sizes sum to 12288.
All inputs are finite; a program needn't handle non-finite values.
Results may differ from a plain program's by a relative error of at most 0.0058.
Values may be sent and summed in bfloat16 or wider, within the bound.
No kernel may reach another device: no remote copies, remote signals or barrier semaphores. Data moves between devices by JAX's collectives and lax.ppermute only.
A program may use at most 64 MiB of HBM per device.

v0:
```python
import jax
import jax.numpy as jnp
from jax import lax
from jax.sharding import PartitionSpec as P

G = 4


def swapped(array, axis, stride):
    return lax.ppermute(array, axis, [(i, i ^ 1 << stride) for i in range(lax.axis_size(axis))])


def on_device(theta, env_left, env_right, mpo_core, sector_sizes):
    sectors = theta.shape[0]
    rows_local = theta.shape[1]
    width = theta.shape[2]
    local_w = env_left.shape[0]
    slab = env_left.shape[1]
    sec_place = lax.axis_index("sec")
    sector = sec_place // G
    block_pos = sec_place % G
    live_size = jnp.sum(jnp.where(jnp.arange(sectors, dtype=jnp.int32) == sector, sector_sizes, 0))
    bit_count = G.bit_length() - 1
    spread = jnp.broadcast_to(theta[:, None], (sectors, G, rows_local, width))
    spread = spread.reshape(sectors * G, rows_local, width)
    sector_block = lax.all_to_all(spread, "sec", split_axis=0, concat_axis=1, tiled=True)[0]
    positions = jnp.arange(width, dtype=jnp.int32)
    keep_row = positions < live_size
    sector_block = jnp.where(
        keep_row[:, None] & keep_row[None, :], sector_block, jnp.zeros_like(sector_block)
    )
    product = jnp.einsum(
        "akm,mn->akn", env_left, sector_block, preferred_element_type=jnp.float32
    ).astype(jnp.bfloat16)
    own_start = lax.axis_index("mpo") * local_w
    core_cols = lax.dynamic_slice_in_dim(mpo_core, own_start, local_w, 1)
    mixed = jnp.einsum(
        "ab,akn->bkn",
        core_cols,
        lax.all_gather(product, "mpo", axis=0, tiled=True).astype(jnp.float32),
        precision=lax.Precision.HIGHEST,
    ).astype(jnp.bfloat16)
    for bit_index in range(bit_count):
        partner = swapped(mixed, "sec", bit_index)
        upper_half = sec_place >> bit_index & 1 == 1
        mixed = jnp.where(
            upper_half, jnp.concatenate([partner, mixed], 1), jnp.concatenate([mixed, partner], 1)
        )
    col_keep = block_pos * slab + jnp.arange(slab, dtype=jnp.int32) < live_size
    sector_term = jnp.einsum("bil,bjl->ij", mixed, env_right, preferred_element_type=jnp.float32)
    row_keep = (
        jnp.arange(lax.axis_size("mpo") * (width // lax.axis_size("mpo")), dtype=jnp.int32)
        < live_size
    )
    result = lax.psum_scatter(
        jnp.where(row_keep[:, None] & col_keep[None, :], sector_term, jnp.zeros_like(sector_term)),
        "mpo",
        scatter_dimension=0,
        tiled=True,
    )
    return result.astype(jnp.bfloat16)


def solution(mesh):
    return jax.shard_map(
        on_device,
        mesh=mesh,
        in_specs=(P(None, "sec", None), P("mpo", "sec", None), P("mpo", "sec", None), P(), P()),
        out_specs=P("mpo", "sec"),
        check_vma=False,
    )
```

profile of v0, /device:TPU:2, one launch (start us, length us, event | category | flops | bytes accessed | tf_op | source)
XLA Modules:
  0.0 477.4 jit_solution(1534336615428155424)
XLA Ops:
  6.5 0.0 copy-start
  6.5 0.0 copy-start.7
  6.5 2.8 broadcast_in_dim.11
  9.3 18.8 %all-to-all-start = ((bf16[64,16,1024]{2,1,0:T(8,128)(2,1)}), bf16[64,16,1024]{2,1,0:T(8,128)(2,1)}, u32[]{:S(2)}, u32[]{:S(2)}) async-start(bf16[64,16,1024]{2,1,0:T(8,128)(2,1)} %bitcast.21), calls=%async_computation | async-start | bytes 4194304 | tf_op jit(solution)/shard_map/all_to_all | solution.py:26
  28.1 0.0 all-gather.2.cloned.1.call-start
  28.2 0.0 copy-done.7
  28.2 0.6 fusion.27
  28.8 0.6 iota_compare_fusion
  29.5 95.7 %all-to-all-done = bf16[64,16,1024]{2,1,0:T(8,128)(2,1)} async-done(((bf16[64,16,1024]{2,1,0:T(8,128)(2,1)}), bf16[64,16,1024]{2,1,0:T(8,128)(2,1)}, u32[]{:S(2)}, u32[]{:S(2)}) %all-to-all-start) | async-done | bytes 2097184 | tf_op jit(solution)/shard_map/all_to_all | solution.py:26
  125.2 0.0 copy-done
  125.2 0.0 copy-start.5
  125.2 4.9 %fusion.15 = bf16[3,256,1024]{2,1,0:T(8,128)(2,1)} fusion(bf16[3,256,1024]{2,1,0:T(8,128)(2,1)S(1)} %copy-done, bf16[1024,1024]{1,0:T(8,128)(2,1)} %bitcast.2, pred[1024]{0:T(1024)(128)(4,1)S(1)} %iota_compare_fusion), kind=kOutput, calls=%fused_computation.13 | convolution fusion | flops 1613496320 | bytes 5243904 | tf_op jit(solution)/shard_map/akm,mn->akn/dot_general | solution.py:32
  130.1 0.0 all-gather.2.cloned.1.call-update
  130.1 0.0 reduce-scatter.2.cloned.1.call-start
  130.2 69.3 %all-gather.2.cloned.1.call-done = bf16[24,256,1024]{2,1,0:T(8,128)(2,1)} async-done(((bf16[3,256,1024]{2,1,0:T(8,128)(2,1)}), bf16[24,256,1024]{2,1,0:T(8,128)(2,1)}) %all-gather.2.cloned.1.call-update) | async-done | bytes 12582928 | tf_op jit(solution)/shard_map/all_gather | solution.py:40
  199.5 0.0 copy-done.5
  199.5 17.3 %fusion.9 = bf16[3,256,1024]{2,0,1:T(4,128)(2,1)S(1)} fusion(bf16[24,256,1024]{2,1,0:T(8,128)(2,1)} %all-gather.2.cloned.1.call-done, f32[24,24]{1,0:T(8,128)S(1)} %copy-done.5, s32[]{:T(128)S(6)} %select_n.47), kind=kOutput, calls=%fused_computation.11 | convolution fusion | flops 227278848 | bytes 14158084 | tf_op jit(solution)/shard_map/ab,akn->bkn/dot_general | solution.py:37
  216.8 0.0 copy-start.3
  216.8 1.3 copy-done.3
  218.1 1.8 copy.10
  219.8 3.6 collective-permute-start
  223.5 0.0 copy-start.4
  223.5 35.0 %collective-permute-done = bf16[3,256,1024]{2,1,0:T(8,128)(2,1)S(1)} collective-permute-done((bf16[3,256,1024]{2,1,0:T(8,128)(2,1)}, bf16[3,256,1024]{2,1,0:T(8,128)(2,1)S(1)}, u32[]{:S(2)}, u32[]{:S(2)}) %collective-permute-start) | collective-permute-done | bytes 1572896 | tf_op jit(solution)/shard_map/ppermute | solution.py:10
  258.5 1.4 copy.11
  259.8 0.0 copy-done.4
  259.9 4.7 maximum_select_fusion.1
  264.5 0.0 copy-start.1
  264.5 1.9 copy-done.1
  266.5 2.9 copy.13
  269.4 4.4 collective-permute-start.1
  273.9 0.0 copy-start.2
  273.9 0.8 add_compare_fusion
  274.7 134.6 %collective-permute-done.1 = bf16[3,512,1024]{2,1,0:T(8,128)(2,1)} collective-permute-done((bf16[3,512,1024]{2,1,0:T(8,128)(2,1)}, bf16[3,512,1024]{2,1,0:T(8,128)(2,1)}, u32[]{:S(2)}, u32[]{:S(2)}) %collective-permute-start.1) | collective-permute-done | bytes 3145760 | tf_op jit(solution)/shard_map/ppermute | solution.py:10
  409.3 4.6 copy.14
  413.9 0.0 copy-done.2
  413.9 0.0 copy-start.6
  413.9 9.3 %maximum_select_fusion = bf16[3,1024,1024]{2,0,1:T(4,128)(2,1)S(1)} fusion(bf16[3,512,1024]{2,0,1:T(4,128)(2,1)S(1)} %copy-done.2, bf16[3,512,1024]{2,0,1:T(4,128)(2,1)S(1)} %copy.14, pred[]{:T(512)S(6)} %eq.16), kind=kLoop, calls=%fused_computation.2 | loop fusion | flops 9437184 | bytes 12582913 | tf_op jit(solution)/shard_map/jit(_where)/select_n | solution.py:46
  423.3 0.0 copy-done.6
  423.3 5.2 %fusion.21 = f32[1024,256]{1,0:T(8,128)} fusion(bf16[3,256,1024]{2,1,0:T(8,128)(2,1)S(1)} %copy-done.6, bf16[3,1024,1024]{2,0,1:T(4,128)(2,1)S(1)} %maximum_select_fusion, pred[256]{0:T(512)(128)(4,1)S(1)} %add_compare_fusion, pred[1024]{0:T(1024)(128)(4,1)S(1)} %iota_compare_fusion), kind=kOutput, calls=%fused_computation.15 | convolution fusion | flops 1611137024 | bytes 8914176 | tf_op jit(solution)/shard_map/bil,bjl->ij/dot_general | solution.py:50
  428.5 0.0 reduce-scatter.2.cloned.1.call-update
  428.5 40.5 %reduce-scatter.2.cloned.1.call-done = f32[128,256]{1,0:T(8,128)} async-done(((f32[1024,256]{1,0:T(8,128)}), f32[128,256]{1,0:T(8,128)}) %reduce-scatter.2.cloned.1.call-update) | async-done | bytes 131088 | tf_op jit(solution)/shard_map/reduce_scatter | solution.py:55
  469.0 1.5 convert_element_type.16
Async XLA Ops:
  6.5 118.7 %copy-start = (bf16[3,256,1024]{2,1,0:T(8,128)(2,1)S(1)}, bf16[3,256,1024]{2,1,0:T(8,128)(2,1)}, u32[]{:S(2)}) copy-start(bf16[3,256,1024]{2,1,0:T(8,128)(2,1)} %param.6) | copy-start | bytes 4718596
  6.5 21.7 %copy-start.7 = (s32[16]{0:T(128)S(1)}, s32[16]{0:T(128)}, u32[]{:S(2)}) copy-start(s32[16]{0:T(128)} %param.9) | copy-start | bytes 196
  9.3 115.9 %all-to-all-start = ((bf16[64,16,1024]{2,1,0:T(8,128)(2,1)}), bf16[64,16,1024]{2,1,0:T(8,128)(2,1)}, u32[]{:S(2)}, u32[]{:S(2)}) async-start(bf16[64,16,1024]{2,1,0:T(8,128)(2,1)} %bitcast.21), calls=%async_computation | async-start | bytes 4194304 | tf_op jit(solution)/shard_map/all_to_all | solution.py:26
  28.1 171.4 %all-gather.2.cloned.1.call-start = ((), (), s32[]{:S(2)}) async-start(), calls=%async_computation.2 | async-start | bytes 14155776 | tf_op jit(solution)/shard_map/all_gather | solution.py:40
  125.2 74.3 %copy-start.5 = (f32[24,24]{1,0:T(8,128)S(1)}, f32[24,24]{1,0:T(8,128)}, u32[]{:S(2)}) copy-start(f32[24,24]{1,0:T(8,128)} %param.8) | copy-start | bytes 6916
  130.1 338.9 %reduce-scatter.2.cloned.1.call-start = ((), (), s32[]{:S(2)}) async-start(), calls=%async_computation.3 | async-start | bytes 1179648 | tf_op jit(solution)/shard_map/reduce_scatter | solution.py:55
  216.8 1.3 copy-start.3
  219.8 38.6 %collective-permute-start = (bf16[3,256,1024]{2,1,0:T(8,128)(2,1)}, bf16[3,256,1024]{2,1,0:T(8,128)(2,1)S(1)}, u32[]{:S(2)}, u32[]{:S(2)}) collective-permute-start(bf16[3,256,1024]{2,1,0:T(8,128)(2,1)} %copy.10), channel_id=1, source_target_pairs={{0,1},{1,0},{2,3},{3,2},{4,5},{5,4},{6,7},{7,6},{8,9},{9,8},{10,11... | collective-permute-start | bytes 4718600 | tf_op jit(solution)/shard_map/ppermute | solution.py:10
  223.5 36.4 %copy-start.4 = (bf16[3,256,1024]{2,0,1:T(4,128)(2,1)S(1)}, bf16[3,256,1024]{2,0,1:T(4,128)(2,1)}, u32[]{:S(2)}) copy-start(bf16[3,256,1024]{2,0,1:T(4,128)(2,1)} %copy-done.3) | copy-start | bytes 4718596
  264.5 2.0 copy-start.1
  269.4 139.9 %collective-permute-start.1 = (bf16[3,512,1024]{2,1,0:T(8,128)(2,1)}, bf16[3,512,1024]{2,1,0:T(8,128)(2,1)}, u32[]{:S(2)}, u32[]{:S(2)}) collective-permute-start(bf16[3,512,1024]{2,1,0:T(8,128)(2,1)} %copy.13), channel_id=1, source_target_pairs={{0,2},{1,3},{2,0},{3,1},{4,6},{5,7},{6,4},{7,5},{8,10},{9,11},{10,... | collective-permute-start | bytes 9437192 | tf_op jit(solution)/shard_map/ppermute | solution.py:10
  273.9 140.0 %copy-start.2 = (bf16[3,512,1024]{2,0,1:T(4,128)(2,1)S(1)}, bf16[3,512,1024]{2,0,1:T(4,128)(2,1)}, u32[]{:S(2)}) copy-start(bf16[3,512,1024]{2,0,1:T(4,128)(2,1)} %copy-done.1) | copy-start | bytes 9437188
  413.9 9.3 %copy-start.6 = (bf16[3,256,1024]{2,1,0:T(8,128)(2,1)S(1)}, bf16[3,256,1024]{2,1,0:T(8,128)(2,1)}, u32[]{:S(2)}) copy-start(bf16[3,256,1024]{2,1,0:T(8,128)(2,1)} %param.7) | copy-start | bytes 4718596
Sparse Core Ops, SparseCore 0:
  130.3 69.1 all-gather.1
  428.7 40.3 reduce-scatter.1
where the time goes:
time: 478 us; the launch traced here: 477 us
  waiting for transfers between devices  375 us (78%)
  matrix products  27.4 us (6%)
  starting transfers between devices  27 us (6%)
  other arithmetic  17.6 us (4%)
  local copies, waits for them, and re-layouts  16.7 us (3%)
  between operations  13.6 us (3%)
    ppermute x2, waiting for transfers between devices, swapped(): lax.ppermute(array, axis, [(i, i ^ 1 << stride) for i in range(lax.axis_s...  170 us
    all_to_all x1, waiting for transfers between devices, on_device(): lax.all_to_all(spread, 'sec', split_axis=0, concat_axis=1, tiled=True)[0]  95.7 us
    all_gather x1, waiting for transfers between devices, on_device(): lax.all_gather(product, 'mpo', axis=0, tiled=True).astype(jnp.float32)  69.3 us
    reduce_scatter x1, waiting for transfers between devices, on_device(): lax.psum_scatter(jnp.where(row_keep[:, None] & col_keep[None, :], sector_...  40.5 us
    all_to_all x1, starting transfers between devices, on_device(): lax.all_to_all(spread, 'sec', split_axis=0, concat_axis=1, tiled=True)[0]  18.8 us
    dot_general x1, matrix products, on_device(): jnp.einsum('ab,akn->bkn', core_cols, lax.all_gather(product, 'mpo', axis=...  17.3 us
    select_n x2, other arithmetic, on_device(): jnp.where(upper_half, jnp.concatenate([partner, mixed], 1), jnp.concatena...  14 us
  transfers between devices with their start and end apart: 5, of which 5 were waited for; matrix products, arithmetic and copies ran while one was open for 0% of the time, Pallas kernels for 0%

commit v1 on v0

--- a/solution.py
+++ b/solution.py
@@ -4,6 +4,26 @@
 from jax.sharding import PartitionSpec as P
 
 G = 4
+
+
+def knots_supply_all(v0, device_axis):
+    n_blocks = lax.psum(1, device_axis)
+    all_blocks = []
+    for nth in [*range(n_blocks)]:
+        all_blocks.append((nth, (nth + 1) % n_blocks))
+    history = []
+    for nth in [*range(n_blocks)]:
+        history.append((nth, (nth - 1) % n_blocks))
+    out_arr, everything = ([v0], [v0])
+    for _ in range(n_blocks // 2):
+        res = lax.ppermute(out_arr[-1], device_axis, all_blocks)
+        out_arr.append(res)
+    for _ in tuple(range((n_blocks - 1) // 2)):
+        main = lax.ppermute(everything[-1], device_axis, history)
+        everything.append(main)
+    ready = jnp.concatenate([*out_arr[::-1], *everything[1:]], 0)
+    next_value = lax.axis_index(device_axis)
+    return jnp.roll(ready, (next_value - n_blocks // 2) * v0.shape[0], 0)
 
 
 def swapped(array, axis, stride):
@@ -37,7 +57,7 @@
     mixed = jnp.einsum(
         "ab,akn->bkn",
         core_cols,
-        lax.all_gather(product, "mpo", axis=0, tiled=True).astype(jnp.float32),
+        knots_supply_all(product, "mpo").astype(jnp.float32),
         precision=lax.Precision.HIGHEST,
     ).astype(jnp.bfloat16)
     for bit_index in range(bit_count):

time: 478 us -> 509 us (1.065)
  the two profiles are of different devices: /device:TPU:2 before, /device:TPU:4 now
where the time goes in v1:
time: 509 us; the launch traced here: 508 us
  waiting for transfers between devices  369 us (72%)
  local copies, waits for them, and re-layouts  51.3 us (10%)
  starting transfers between devices  36.7 us (7%)
  other arithmetic  19 us (4%)
  matrix products  17.8 us (3%)
  between operations  13.7 us (3%)
    ppermute x2, waiting for transfers between devices, swapped(): lax.ppermute(array, axis, [(i, i ^ 1 << stride) for i in range(lax.axis_s...  158 us
    all_to_all x1, waiting for transfers between devices, on_device(): lax.all_to_all(spread, 'sec', split_axis=0, concat_axis=1, tiled=True)[0]  95.9 us
    ppermute x4, waiting for transfers between devices, knots_supply_all(): res = lax.ppermute(out_arr[-1], device_axis, all_blocks)  73.4 us
    reduce_scatter x1, waiting for transfers between devices, on_device(): lax.psum_scatter(jnp.where(row_keep[:, None] & col_keep[None, :], sector_...  41.2 us
    dynamic_slice x2, local copies, waits for them, and re-layouts, knots_supply_all(): return jnp.roll(ready, (next_value - n_blocks // 2) * v0.shape[0], 0)  21.5 us
    all_to_all x1, starting transfers between devices, on_device(): lax.all_to_all(spread, 'sec', split_axis=0, concat_axis=1, tiled=True)[0]  18.9 us
    unnamed x39, local copies, waits for them, and re-layouts  16 us
    select_n x2, other arithmetic, on_device(): jnp.where(upper_half, jnp.concatenate([partner, mixed], 1), jnp.concatena...  15.3 us
  transfers between devices with their start and end apart: 11, of which 9 were waited for; matrix products, arithmetic and copies ran while one was open for 1% of the time, Pallas kernels for 0%

profile of v1, /device:TPU:4, one launch (start us, length us, event | category | flops | bytes accessed | tf_op | source)
XLA Modules:
  0.0 507.8 jit_solution(12060296069272991342)
XLA Ops:
  6.5 0.0 copy-start
  6.5 2.8 broadcast_in_dim.11
  9.3 18.9 %all-to-all-start = ((bf16[64,16,1024]{2,1,0:T(8,128)(2,1)}), bf16[64,16,1024]{2,1,0:T(8,128)(2,1)}, u32[]{:S(2)}, u32[]{:S(2)}) async-start(bf16[64,16,1024]{2,1,0:T(8,128)(2,1)} %bitcast.22), calls=%async_computation | async-start | bytes 4194304 | tf_op jit(solution)/shard_map/all_to_all | solution.py:46
  28.2 0.0 reduce-scatter.2.cloned.1.call-start
  28.3 0.0 copy-done.11
  28.3 0.6 fusion.22
  28.9 0.6 iota_compare_fusion
  29.6 95.9 %all-to-all-done = bf16[64,16,1024]{2,1,0:T(8,128)(2,1)} async-done(((bf16[64,16,1024]{2,1,0:T(8,128)(2,1)}), bf16[64,16,1024]{2,1,0:T(8,128)(2,1)}, u32[]{:S(2)}, u32[]{:S(2)}) %all-to-all-start) | async-done | bytes 2097184 | tf_op jit(solution)/shard_map/all_to_all | solution.py:46
  125.5 0.0 copy-done
  125.5 3.6 fusion.10
  129.1 0.0 collective-permute-start
  129.1 21.0 %collective-permute-done = bf16[3,256,1024]{1,2,0:T(8,128)(2,1)S(1)} collective-permute-done((bf16[3,256,1024]{1,2,0:T(8,128)(2,1)S(1)}, bf16[3,256,1024]{1,2,0:T(8,128)(2,1)S(1)}, u32[]{:S(2)}, u32[]{:S(2)}) %collective-permute-start) | collective-permute-done | bytes 1572896 | tf_op jit(solution)/shard_map/ppermute | solution.py:19
  150.2 0.0 collective-permute-start.1
  150.2 3.0 collective-permute-start.4
  153.1 18.1 %collective-permute-done.1 = bf16[3,256,1024]{1,2,0:T(8,128)(2,1)S(1)} collective-permute-done((bf16[3,256,1024]{1,2,0:T(8,128)(2,1)S(1)}, bf16[3,256,1024]{1,2,0:T(8,128)(2,1)S(1)}, u32[]{:S(2)}, u32[]{:S(2)}) %collective-permute-start.1) | collective-permute-done | bytes 1572896 | tf_op jit(solution)/shard_map/ppermute | solution.py:19
  171.2 0.0 collective-permute-start.2
  171.2 0.0 collective-permute-done.4
  171.2 1.2 copy-done.5
  172.4 2.9 collective-permute-start.5
  175.3 17.0 %collective-permute-done.2 = bf16[3,256,1024]{1,2,0:T(8,128)(2,1)} collective-permute-done((bf16[3,256,1024]{1,2,0:T(8,128)(2,1)S(1)}, bf16[3,256,1024]{1,2,0:T(8,128)(2,1)}, u32[]{:S(2)}, u32[]{:S(2)}) %collective-permute-start.2) | collective-permute-done | bytes 1572896 | tf_op jit(solution)/shard_map/ppermute | solution.py:19
  192.4 0.0 collective-permute-start.3
  192.4 0.9 collective-permute-done.5
  193.3 3.2 collective-permute-start.6
  196.5 17.3 %collective-permute-done.3 = bf16[3,256,1024]{1,2,0:T(8,128)(2,1)} collective-permute-done((bf16[3,256,1024]{1,2,0:T(8,128)(2,1)}, bf16[3,256,1024]{1,2,0:T(8,128)(2,1)}, u32[]{:S(2)}, u32[]{:S(2)}) %collective-permute-start.3) | collective-permute-done | bytes 1572896 | tf_op jit(solution)/shard_map/ppermute | solution.py:19
  213.8 1.5 constant_dynamic-update-slice_fusion.15
  215.3 1.6 constant_dynamic-update-slice_fusion.14
  216.9 0.1 constant_dynamic-update-slice_fusion.13
  217.0 0.1 constant_dynamic-update-slice_fusion.12
  217.1 0.1 constant_dynamic-update-slice_fusion.11
  217.3 0.1 constant_dynamic-update-slice_fusion.10
  217.4 1.5 constant_dynamic-update-slice_fusion.9
  218.9 0.0 collective-permute-done.6
  218.9 1.5 constant_dynamic-update-slice_fusion.8
  220.4 1.5 constant_dynamic-update-slice_fusion.7
  221.9 1.5 constant_dynamic-update-slice_fusion.6
  223.4 0.1 constant_dynamic-update-slice_fusion.5
  223.6 0.1 constant_dynamic-update-slice_fusion.4
  223.7 0.1 constant_dynamic-update-slice_fusion.3
  223.8 0.1 constant_dynamic-update-slice_fusion.2
  223.9 1.5 constant_dynamic-update-slice_fusion.1
  225.4 1.5 constant_dynamic-update-slice_fusion
  226.9 5.1 %constant_dynamic-slice_fusion = bf16[24,256,1024]{1,2,0:T(8,128)(2,1)} fusion(bf16[48,256,1024]{1,2,0:T(8,128)(2,1)S(1)} %constant_dynamic-update-slice_fusion, s32[]{:T(128)S(6)} %select_n.62), kind=kLoop, calls=%fused_computation.37 | loop fusion | bytes 25165828 | tf_op jit(solution)/shard_map/jit(_roll_dynamic)/dynamic_slice | solution.py:26
  232.0 16.4 %copy.16 = bf16[24,256,1024]{2,0,1:T(8,128)(2,1)} copy(bf16[24,256,1024]{1,2,0:T(8,128)(2,1)} %constant_dynamic-slice_fusion) | data formatting | bytes 25165824 | tf_op jit(solution)/shard_map/jit(_roll_dynamic)/dynamic_slice | solution.py:26
  248.5 8.9 %convolution_convert_fusion = bf16[3,256,1024]{2,0,1:T(4,128)(2,1)S(1)} fusion(bf16[24,256,1024]{2,0,1:T(8,128)(2,1)} %copy.16, f32[24,24]{1,0:T(8,128)S(1)} %copy-done.9, s32[]{:T(128)S(6)} %select_n.59), kind=kOutput, calls=%fused_computation.9 | convolution fusion | flops 227278848 | bytes 14158084 | tf_op jit(solution)/shard_map/ab,akn->bkn/dot_general | solution.py:57
  257.4 1.3 copy-done.4
  258.7 0.6 copy.17
  259.3 4.4 collective-permute-start.7
  263.7 28.7 %collective-permute-done.7 = bf16[3,256,1024]{2,1,0:T(8,128)(2,1)S(1)} collective-permute-done((bf16[3,256,1024]{2,1,0:T(8,128)(2,1)S(1)}, bf16[3,256,1024]{2,1,0:T(8,128)(2,1)S(1)}, u32[]{:S(2)}, u32[]{:S(2)}) %collective-permute-start.7) | collective-permute-done | bytes 1572896 | tf_op jit(solution)/shard_map/ppermute | solution.py:30
  292.4 1.4 copy.18
  293.8 6.0 %maximum_select_fusion.1 = bf16[3,512,1024]{2,0,1:T(4,128)(2,1)S(1)} fusion(bf16[3,256,1024]{2,0,1:T(4,128)(2,1)} %copy-done.4, bf16[3,256,1024]{2,0,1:T(4,128)(2,1)S(1)} %copy.18, pred[]{:T(512)S(6)} %eq.20), kind=kLoop, calls=%fused_computation.3 | loop fusion | flops 4718592 | bytes 6291457 | tf_op jit(solution)/shard_map/jit(_where)/select_n | solution.py:66
  299.8 1.9 copy-done.2
  301.7 2.9 copy.20
  304.7 4.3 collective-permute-start.8
  309.0 0.8 add_compare_fusion
  309.8 129.2 %collective-permute-done.8 = bf16[3,512,1024]{2,1,0:T(8,128)(2,1)} collective-permute-done((bf16[3,512,1024]{2,1,0:T(8,128)(2,1)}, bf16[3,512,1024]{2,1,0:T(8,128)(2,1)}, u32[]{:S(2)}, u32[]{:S(2)}) %collective-permute-start.8) | collective-permute-done | bytes 3145760 | tf_op jit(solution)/shard_map/ppermute | solution.py:30
  439.0 4.6 copy.21
  443.6 0.0 copy-start.10
  443.6 0.0 copy-start.1
  443.6 9.3 %maximum_select_fusion = bf16[3,1024,1024]{2,0,1:T(4,128)(2,1)S(1)} fusion(bf16[3,512,1024]{2,0,1:T(4,128)(2,1)S(1)} %copy-done.3, bf16[3,512,1024]{2,0,1:T(4,128)(2,1)S(1)} %copy.21, pred[]{:T(512)S(6)} %eq.19), kind=kLoop, calls=%fused_computation | loop fusion | flops 9437184 | bytes 12582913 | tf_op jit(solution)/shard_map/jit(_where)/select_n | solution.py:66
  452.9 0.0 copy-done.10
  452.9 5.2 %fusion.16 = f32[1024,256]{1,0:T(8,128)} fusion(bf16[3,256,1024]{2,1,0:T(8,128)(2,1)S(1)} %copy-done.10, bf16[3,1024,1024]{2,0,1:T(4,128)(2,1)S(1)} %maximum_select_fusion, pred[256]{0:T(512)(128)(4,1)S(1)} %add_compare_fusion, pred[1024]{0:T(1024)(128)(4,1)S(1)} %iota_compare_fusion), kind=kOutput, calls=%fused_computation.13 | convolution fusion | flops 1611137024 | bytes 8914176 | tf_op jit(solution)/shard_map/bil,bjl->ij/dot_general | solution.py:70
  458.2 0.0 reduce-scatter.2.cloned.1.call-update
  458.2 41.2 %reduce-scatter.2.cloned.1.call-done = f32[128,256]{1,0:T(8,128)} async-done(((f32[1024,256]{1,0:T(8,128)}), f32[128,256]{1,0:T(8,128)}) %reduce-scatter.2.cloned.1.call-update) | async-done | bytes 131088 | tf_op jit(solution)/shard_map/reduce_scatter | solution.py:75
  499.4 1.5 convert_element_type.16
  (15 shorter events, 0.0 us)
Async XLA Ops:
  6.5 118.9 %copy-start = (bf16[3,256,1024]{2,1,0:T(8,128)(2,1)S(1)}, bf16[3,256,1024]{2,1,0:T(8,128)(2,1)}, u32[]{:S(2)}) copy-start(bf16[3,256,1024]{2,1,0:T(8,128)(2,1)} %param.6) | copy-start | bytes 4718596
  6.5 21.7 %copy-start.11 = (s32[16]{0:T(128)S(1)}, s32[16]{0:T(128)}, u32[]{:S(2)}) copy-start(s32[16]{0:T(128)} %param.9) | copy-start | bytes 196
  9.3 116.2 %all-to-all-start = ((bf16[64,16,1024]{2,1,0:T(8,128)(2,1)}), bf16[64,16,1024]{2,1,0:T(8,128)(2,1)}, u32[]{:S(2)}, u32[]{:S(2)}) async-start(bf16[64,16,1024]{2,1,0:T(8,128)(2,1)} %bitcast.22), calls=%async_computation | async-start | bytes 4194304 | tf_op jit(solution)/shard_map/all_to_all | solution.py:46
  28.2 471.2 %reduce-scatter.2.cloned.1.call-start = ((), (), s32[]{:S(2)}) async-start(), calls=%async_computation.2 | async-start | bytes 1179648 | tf_op jit(solution)/shard_map/reduce_scatter | solution.py:75
  129.1 21.1 %collective-permute-start = (bf16[3,256,1024]{1,2,0:T(8,128)(2,1)S(1)}, bf16[3,256,1024]{1,2,0:T(8,128)(2,1)S(1)}, u32[]{:S(2)}, u32[]{:S(2)}) collective-permute-start(bf16[3,256,1024]{1,2,0:T(8,128)(2,1)S(1)} %fusion.10), channel_id=1, source_target_pairs={{0,64},{64,128},{128,192},{192,256},{256,320},{320,384},{384,448},... | collective-permute-start | bytes 4718600 | tf_op jit(solution)/shard_map/ppermute | solution.py:19
  150.2 21.1 %collective-permute-start.1 = (bf16[3,256,1024]{1,2,0:T(8,128)(2,1)S(1)}, bf16[3,256,1024]{1,2,0:T(8,128)(2,1)S(1)}, u32[]{:S(2)}, u32[]{:S(2)}) collective-permute-start(bf16[3,256,1024]{1,2,0:T(8,128)(2,1)S(1)} %collective-permute-done), channel_id=1, source_target_pairs={{0,64},{64,128},{128,192},{192,256},{256,320},{320,384},{384,448},... | collective-permute-start | bytes 4718600 | tf_op jit(solution)/shard_map/ppermute | solution.py:19
  150.2 21.1 %collective-permute-start.4 = (bf16[3,256,1024]{1,2,0:T(8,128)(2,1)S(1)}, bf16[3,256,1024]{1,2,0:T(8,128)(2,1)S(1)}, u32[]{:S(2)}, u32[]{:S(2)}) collective-permute-start(bf16[3,256,1024]{1,2,0:T(8,128)(2,1)S(1)} %fusion.10), channel_id=1, source_target_pairs={{0,448},{64,0},{128,64},{192,128},{256,192},{320,256},{384,320},{4... | collective-permute-start | bytes 4718600 | tf_op jit(solution)/shard_map/ppermute | solution.py:22
  171.2 22.0 %copy-start.7 = (bf16[3,256,1024]{1,2,0:T(8,128)(2,1)}, bf16[3,256,1024]{1,2,0:T(8,128)(2,1)S(1)}, u32[]{:S(2)}) copy-start(bf16[3,256,1024]{1,2,0:T(8,128)(2,1)S(1)} %collective-permute-done.1) | copy-start | bytes 4718596
  171.2 21.2 %collective-permute-start.2 = (bf16[3,256,1024]{1,2,0:T(8,128)(2,1)S(1)}, bf16[3,256,1024]{1,2,0:T(8,128)(2,1)}, u32[]{:S(2)}, u32[]{:S(2)}) collective-permute-start(bf16[3,256,1024]{1,2,0:T(8,128)(2,1)S(1)} %collective-permute-done.1), channel_id=1, source_target_pairs={{0,64},{64,128},{128,192},{192,256},{256,320},{320,384},{384,448},... | collective-permute-start | bytes 4718600 | tf_op jit(solution)/shard_map/ppermute | solution.py:19
  171.2 1.2 copy-start.5
  172.4 20.9 %collective-permute-start.5 = (bf16[3,256,1024]{1,2,0:T(8,128)(2,1)S(1)}, bf16[3,256,1024]{1,2,0:T(8,128)(2,1)}, u32[]{:S(2)}, u32[]{:S(2)}) collective-permute-start(bf16[3,256,1024]{1,2,0:T(8,128)(2,1)S(1)} %collective-permute-done.4), channel_id=1, source_target_pairs={{0,448},{64,0},{128,64},{192,128},{256,192},{320,256},{384,320},{4... | collective-permute-start | bytes 4718600 | tf_op jit(solution)/shard_map/ppermute | solution.py:22
  192.4 21.4 %collective-permute-start.3 = (bf16[3,256,1024]{1,2,0:T(8,128)(2,1)}, bf16[3,256,1024]{1,2,0:T(8,128)(2,1)}, u32[]{:S(2)}, u32[]{:S(2)}) collective-permute-start(bf16[3,256,1024]{1,2,0:T(8,128)(2,1)} %collective-permute-done.2), channel_id=1, source_target_pairs={{0,64},{64,128},{128,192},{192,256},{256,320},{320,384},{384,448},... | collective-permute-start | bytes 4718600 | tf_op jit(solution)/shard_map/ppermute | solution.py:19
  193.3 25.6 %collective-permute-start.6 = (bf16[3,256,1024]{1,2,0:T(8,128)(2,1)}, bf16[3,256,1024]{1,2,0:T(8,128)(2,1)}, u32[]{:S(2)}, u32[]{:S(2)}) collective-permute-start(bf16[3,256,1024]{1,2,0:T(8,128)(2,1)} %collective-permute-done.5), channel_id=1, source_target_pairs={{0,448},{64,0},{128,64},{192,128},{256,192},{320,256},{384,320},{4... | collective-permute-start | bytes 4718600 | tf_op jit(solution)/shard_map/ppermute | solution.py:22
  196.5 20.4 %copy-start.8 = (bf16[3,256,1024]{1,2,0:T(8,128)(2,1)S(1)}, bf16[3,256,1024]{1,2,0:T(8,128)(2,1)}, u32[]{:S(2)}) copy-start(bf16[3,256,1024]{1,2,0:T(8,128)(2,1)} %copy-done.7) | copy-start | bytes 4718596
  215.3 2.0 copy-start.6
  232.0 16.4 %copy-start.9 = (f32[24,24]{1,0:T(8,128)S(1)}, f32[24,24]{1,0:T(8,128)}, u32[]{:S(2)}) copy-start(f32[24,24]{1,0:T(8,128)} %param.8) | copy-start | bytes 6916
  257.4 1.3 copy-start.4
  259.3 33.1 %collective-permute-start.7 = (bf16[3,256,1024]{2,1,0:T(8,128)(2,1)S(1)}, bf16[3,256,1024]{2,1,0:T(8,128)(2,1)S(1)}, u32[]{:S(2)}, u32[]{:S(2)}) collective-permute-start(bf16[3,256,1024]{2,1,0:T(8,128)(2,1)S(1)} %copy.17), channel_id=1, source_target_pairs={{0,1},{1,0},{2,3},{3,2},{4,5},{5,4},{6,7},{7,6},{8,9},{9,8},{10,11... | collective-permute-start | bytes 4718600 | tf_op jit(solution)/shard_map/ppermute | solution.py:30
  299.8 1.9 copy-start.2
  304.7 134.3 %collective-permute-start.8 = (bf16[3,512,1024]{2,1,0:T(8,128)(2,1)}, bf16[3,512,1024]{2,1,0:T(8,128)(2,1)}, u32[]{:S(2)}, u32[]{:S(2)}) collective-permute-start(bf16[3,512,1024]{2,1,0:T(8,128)(2,1)} %copy.20), channel_id=1, source_target_pairs={{0,2},{1,3},{2,0},{3,1},{4,6},{5,7},{6,4},{7,5},{8,10},{9,11},{10,... | collective-permute-start | bytes 9437192 | tf_op jit(solution)/shard_map/ppermute | solution.py:30
  309.0 134.6 %copy-start.3 = (bf16[3,512,1024]{2,0,1:T(4,128)(2,1)S(1)}, bf16[3,512,1024]{2,0,1:T(4,128)(2,1)}, u32[]{:S(2)}) copy-start(bf16[3,512,1024]{2,0,1:T(4,128)(2,1)} %copy-done.2) | copy-start | bytes 9437188
  443.6 9.4 %copy-start.10 = (bf16[3,256,1024]{2,1,0:T(8,128)(2,1)S(1)}, bf16[3,256,1024]{2,1,0:T(8,128)(2,1)}, u32[]{:S(2)}) copy-start(bf16[3,256,1024]{2,1,0:T(8,128)(2,1)} %param.7) | copy-start | bytes 4718596
  443.6 57.3 %copy-start.1 = (bf16[3,256,1024]{2,1,0:T(8,128)(2,1)S(1)}, bf16[3,256,1024]{2,1,0:T(8,128)(2,1)}, u32[]{:S(2)}) copy-start(bf16[3,256,1024]{2,1,0:T(8,128)(2,1)} %param.6) | copy-start | bytes 4718596
Sparse Core Ops, SparseCore 0:
  458.3 41.0 reduce-scatter.1
